TPU v7x, 128 devices: a whole 4x4x4 slice. The times are simulated.
128 devices in a mesh: dp: 4 (over x), seq: 8 (over z, core), expert: 4 (over y).
Axes of the slice: x: 4, y: 4, z: 4, core: 2. Of those that a mesh axis runs over, the one named last changes fastest.
Arguments:
- x_in: bfloat16 [4096, 8192], P(('dp', 'seq'), 'expert'), parts along dimension 0, may hold values from -6 to 6
- z_in: bfloat16 [4096, 8192], P(('dp', 'seq'), 'expert'), parts along dimension 0, may hold values from -6 to 6
- step_raw: bfloat16 [4096, 8192], P(('dp', 'seq'), 'expert'), parts along dimension 0, may hold values from -4 to 4
- step_bias: float32 [8192], P('expert'), may hold values from -9 to -2
- decay_rate: float32 [16, 8192], P(None, 'expert'), may hold values from 0.5 to 4
- b_coef: bfloat16 [16, 4096], P(None, ('dp', 'seq')), parts along dimension 1, may hold values from -6 to 6
- c_coef: bfloat16 [16, 4096], P(None, ('dp', 'seq')), parts along dimension 1, may hold values from -6 to 6
- skip_gain: float32 [8192], P('expert'), may hold values from 0.5 to 1.5
- out_proj: bfloat16 [8192, 8192], P('expert', 'seq'), may hold values from -0.0625 to 0.0625
- residual: bfloat16 [4096, 8192], P(('dp', 'seq', 'expert')), parts along dimension 0, may hold values from -6 to 6
- norm_gain: float32 [8192], replicated, may hold values from 0.5 to 1.5
- router_weight: bfloat16 [8192, 16], replicated, may hold values from -0.0625 to 0.0625
- expert_ids: int32 [4096, 2], P(('dp', 'seq', 'expert')), parts along dimension 0, may hold values from 0 to 15, as said below
- gate_weight: bfloat16 [8192, 12288], P(None, ('seq', 'expert')), may hold values from -0.0625 to 0.0625
- up_weight: bfloat16 [8192, 12288], P(None, ('seq', 'expert')), may hold values from -0.0625 to 0.0625
- down_weight: bfloat16 [12288, 8192], P(('seq', 'expert')), may hold values from -0.0546875 to 0.0546875
Outputs:
- final: bfloat16 [4096, 8192], P(('dp', 'seq', 'expert')), parts along dimension 0
There are 4 independent parts, one for each index of `dp`. A program takes and returns all parts, laid end to end along the dimension named above; an argument that names none is the same for every part. Nothing has to cross between parts.
Inputs may be any that keep to these rules, and one draw needn't show every extreme that they name: `expert_ids`: each token names 2 different experts; among the 32 rows of one device at most 16 name expert 0 and at least one does; on some device exactly 16 do.
All inputs are finite; a program needn't handle non-finite values.
Results may differ from a plain program's by a relative error of at most 0.006.
Values may be sent and summed in bfloat16 or wider, within the bound.
No kernel may reach another device: no remote copies, remote signals or barrier semaphores. Data moves between devices by JAX's collectives and lax.ppermute only.
A program may use at most 192 MiB of HBM per device.

v0:
```python
import jax
import jax.numpy as jnp
from jax import lax
from jax.sharding import PartitionSpec as P

BLOCK = 128


def entering(value, axis, join, neutral):
    count, mine = (lax.axis_size(axis), lax.axis_index(axis))
    pieces = jax.tree.map(lambda part: lax.all_gather(part, axis), value)
    running = jax.tree.map(
        lambda part, zero: jnp.full_like(part, 0) + jnp.asarray(zero, part.dtype), value, neutral
    )

    def hop(position, running):
        longer = join(running, jax.tree.map(lambda part: part[position], pieces))
        return jax.tree.map(lambda new, old: jnp.where(position < mine, new, old), longer, running)

    return lax.fori_loop(0, count - 1, hop, running)


def pair_combine(early, later):
    return (early[0] * later[0], later[0] * early[1] + later[1])


def end_state(step_size, x_float, decay_rate, b_rows):

    def end_advance(state, inputs):
        step_now, x_now, b_now = inputs
        state = (
            jnp.exp(-step_now[None, :] * decay_rate) * state
            + (step_now * x_now)[None, :] * b_now[:, None]
        )
        return (state, None)

    start_state = jnp.zeros(decay_rate.shape, jnp.float32)
    final_state, _ = lax.scan(end_advance, start_state, (step_size, x_float, b_rows), unroll=8)
    return final_state


def scan_outputs(state_in, step_size, x_float, decay_rate, b_rows, c_rows, skip_gain):

    def scan_advance(state, inputs):
        step_now, x_now, b_now, c_now = inputs
        state = (
            jnp.exp(-step_now[None, :] * decay_rate) * state
            + (step_now * x_now)[None, :] * b_now[:, None]
        )
        y_now = jnp.sum(c_now[:, None] * state, axis=0) + skip_gain * x_now
        return (state, y_now)

    _, outputs = lax.scan(scan_advance, state_in, (step_size, x_float, b_rows, c_rows), unroll=8)
    return outputs


def on_device(
    x_in,
    z_in,
    step_raw,
    step_bias,
    decay_rate,
    b_coef,
    c_coef,
    skip_gain,
    out_proj,
    residual,
    norm_gain,
    router_weight,
    expert_ids,
    gate_weight,
    up_weight,
    down_weight,
):
    step_size = jax.nn.softplus(step_raw.astype(jnp.float32) + step_bias[None, :])
    x_float = x_in.astype(jnp.float32)
    b_rows = b_coef.astype(jnp.float32).T
    c_rows = c_coef.astype(jnp.float32).T
    state_end = end_state(step_size, x_float, decay_rate, b_rows)
    decay_end = jnp.exp(-decay_rate * jnp.sum(step_size, axis=0)[None, :])
    identity = (jnp.ones_like(decay_end), jnp.zeros_like(state_end))
    carried = entering((decay_end, state_end), "seq", pair_combine, identity)
    state_in = carried[1]
    scanned = scan_outputs(state_in, step_size, x_float, decay_rate, b_rows, c_rows, skip_gain)
    gated = (scanned * jax.nn.silu(z_in.astype(jnp.float32))).astype(jnp.bfloat16)
    column_part = jnp.dot(
        lax.all_gather(gated, "seq", axis=0, tiled=True),
        out_proj,
        preferred_element_type=jnp.float32,
    )
    seq_count = lax.axis_size("seq")
    expert_count = lax.axis_size("expert")
    rows = residual.shape[0]
    grouped = column_part.reshape(seq_count, expert_count, rows, column_part.shape[1])
    summed = lax.psum_scatter(grouped, "expert", scatter_dimension=1, tiled=True)
    arranged = jnp.transpose(summed[:, 0], (1, 0, 2))
    swapped = lax.all_to_all(arranged, "seq", split_axis=1, concat_axis=1, tiled=True)
    mamba_out = swapped.reshape(rows, -1)
    hidden = (residual.astype(jnp.float32) + mamba_out).astype(jnp.bfloat16)
    hidden_f = hidden.astype(jnp.float32)
    width_d = hidden.shape[1]
    scale_cols = width_d // BLOCK
    normed = (
        hidden_f
        * lax.rsqrt(jnp.mean(hidden_f * hidden_f, axis=-1, keepdims=True) + 1e-05)
        * norm_gain[None, :]
    )
    blocked = normed.reshape(rows, scale_cols, BLOCK)
    scales = (jnp.max(jnp.abs(blocked), axis=-1) / 448.0 + 1e-06).astype(jnp.bfloat16)
    quant = (blocked / scales.astype(jnp.float32)[..., None]).astype(jnp.bfloat16)
    restored = (
        (quant.astype(jnp.float32) * scales.astype(jnp.float32)[..., None])
        .astype(jnp.bfloat16)
        .reshape(rows, width_d)
    )
    experts = router_weight.shape[1]
    probs = jax.nn.sigmoid(jnp.dot(restored, router_weight, preferred_element_type=jnp.float32))
    picks = expert_ids[:, :, None] == jnp.arange(experts, dtype=jnp.int32)[None, None, :]
    chosen = jnp.sum(jnp.where(picks, probs[:, None, :], jnp.float32(0.0)), axis=-1)
    weights = chosen / jnp.sum(chosen, axis=-1, keepdims=True)
    coef = jnp.sum(jnp.where(expert_ids == 0, weights, jnp.float32(0.0)), axis=1)
    wanted = jnp.any(expert_ids == 0, axis=1)
    wanted_int = wanted.astype(jnp.int32)
    slot_pos = jnp.cumsum(wanted_int) - wanted_int
    capacity = rows // 2
    table = (
        (slot_pos[None, :] == jnp.arange(capacity, dtype=jnp.int32)[:, None]) & wanted[None, :]
    ).astype(jnp.bfloat16)
    send_quant = jnp.dot(
        table, quant.reshape(rows, width_d), preferred_element_type=jnp.float32
    ).astype(jnp.bfloat16)
    send_scale = jnp.dot(table, scales, preferred_element_type=jnp.float32).astype(jnp.bfloat16)
    all_quant, all_scale = (
        lax.all_gather(send_quant, ("seq", "expert"), axis=0, tiled=True),
        lax.all_gather(send_scale, ("seq", "expert"), axis=0, tiled=True),
    )
    slots = all_quant.shape[0]
    inputs = (
        (
            all_quant.reshape(slots, scale_cols, BLOCK).astype(jnp.float32)
            * all_scale.astype(jnp.float32)[..., None]
        )
        .astype(jnp.bfloat16)
        .reshape(slots, width_d)
    )
    gate_value = jnp.dot(inputs, gate_weight, preferred_element_type=jnp.float32)
    up_value = jnp.dot(inputs, up_weight, preferred_element_type=jnp.float32)
    active = (jax.nn.silu(gate_value) * up_value).astype(jnp.bfloat16)
    own_sum = lax.psum_scatter(
        jnp.dot(active, down_weight, preferred_element_type=jnp.float32).astype(jnp.bfloat16),
        ("seq", "expert"),
        scatter_dimension=0,
        tiled=True,
    )
    returned = jnp.dot(table.T, own_sum, preferred_element_type=jnp.float32)
    return (hidden_f + coef[:, None] * returned).astype(jnp.bfloat16)


def solution(mesh):
    return jax.shard_map(
        on_device,
        mesh=mesh,
        in_specs=(
            P(("dp", "seq"), "expert"),
            P(("dp", "seq"), "expert"),
            P(("dp", "seq"), "expert"),
            P("expert"),
            P(None, "expert"),
            P(None, ("dp", "seq")),
            P(None, ("dp", "seq")),
            P("expert"),
            P("expert", "seq"),
            P(("dp", "seq", "expert"), None),
            P(),
            P(),
            P(("dp", "seq", "expert"), None),
            P(None, ("seq", "expert")),
            P(None, ("seq", "expert")),
            P(("seq", "expert"), None),
        ),
        out_specs=P(("dp", "seq", "expert"), None),
        check_vma=False,
    )
```

profile of v0, /device:TPU:0, one launch (start us, length us, event | category | flops | bytes accessed | tf_op | source)
XLA Modules:
  0.0 533.8 jit_solution(4677953557653513335)
XLA Ops:
  8.5 1.7 fusion.67
  10.2 21.8 %while.38 = (s32[]{:T(128)}, f32[16,2048]{1,0:T(8,128)S(1)}, f32[16,8,2048]{2,1,0:T(8,128)S(1)}, f32[16,2048]{1,0:T(8,128)}, f32[16,8,2048]{2,1,0:T(8,128)S(1)},...) while((s32[]{:T(128)}, f32[16,2048]{1,0:T(8,128)S(1)}, ...), condition=%wide.region_2.3_spmd.clone, body=%wide.region_1.2_spmd.clone.sunk | while | flops 1114122 | bytes 789271 | solution.py:38
  32.8 1.6 multiply_exponential_fusion
  34.6 24.2 %all-gather.13.cloned.1.call-done = f32[128,2048]{1,0:T(8,128)} async-done(((f32[16,2048]{1,0:T(8,128)}), f32[128,2048]{1,0:T(8,128)}) %all-gather.13.cloned.1.call-update) | async-done | bytes 1048592 | tf_op jit(solution)/shard_map/all_gather | solution.py:11
  58.8 25.1 %all-gather.11.cloned.1.call-done = f32[128,2048]{1,0:T(8,128)} async-done(((f32[16,2048]{1,0:T(8,128)}), f32[128,2048]{1,0:T(8,128)}) %all-gather.11.cloned.1.call-update) | async-done | bytes 1048592 | tf_op jit(solution)/shard_map/all_gather | solution.py:11
  84.0 7.6 %while.39 = (s32[]{:T(128)}, f32[16,2048]{1,0:T(8,128)S(1)}, s32[]{:T(128)}, f32[8,16,2048]{2,1,0:T(8,128)}, f32[8,16,2048]{2,1,0:T(8,128)}, /*index=5*/s32[]{:T(128)}, s32[]{:T(128)}) while((s32[]{:T(128)}, f32[16,2048]{1,0:T(8,128)S(1)}, s32[]{:T(128)}, f32[8,16,2048]{2,1,0:T(8,128)}, f32[8,16,2048]{2,1,0:T(8,128)}, ...), condition=%wide.region_4.5_spmd.clone, body=%wide.region_3.4_spmd.clone.sunk | while | flops 131076 | bytes 524397 | solution.py:20
  91.6 71.2 %while.37 = (s32[]{:T(128)}, f32[16,2048]{1,0:T(8,128)S(1)}, f32[16,8,2048]{2,1,0:T(8,128)}, f32[16,8,2048]{2,1,0:T(8,128)S(1)}, f32[16,2048]{1,0:T(8,128)}, /*i...) while((s32[]{:T(128)}, f32[16,2048]{1,0:T(8,128)S(1)}, ...), condition=%wide.region_14.15_spmd, body=%wide.region_5.14_spmd.sunk | while | flops 2408457 | bytes 2078409 | solution.py:53
  97.3 1.2 multiply_reduce_fusion.11
  106.2 1.2 multiply_reduce_fusion.11
  110.7 1.2 multiply_reduce_fusion.11
  119.6 1.2 multiply_reduce_fusion.11
  124.0 1.2 multiply_reduce_fusion.11
  128.5 1.2 multiply_reduce_fusion.11
  132.9 1.2 multiply_reduce_fusion.11
  137.4 1.2 multiply_reduce_fusion.11
  141.8 1.2 multiply_reduce_fusion.11
  150.7 1.2 multiply_reduce_fusion.11
  159.6 1.2 multiply_reduce_fusion.11
  162.8 2.3 fusion.66
  165.2 32.3 %all-gather.7.cloned.1.call-done = bf16[1024,2048]{1,0:T(8,128)(2,1)} async-done(((bf16[128,2048]{1,0:T(8,128)(2,1)}), bf16[1024,2048]{1,0:T(8,128)(2,1)}) %all-gather.7.cloned.1.call-update) | async-done | bytes 4194320 | tf_op jit(solution)/shard_map/all_gather | solution.py:87
  197.5 9.9 %fusion.91 = f32[1024,1024]{1,0:T(8,128)} fusion(bf16[1024,2048]{1,0:T(8,128)(2,1)} %all-gather.7.cloned.1.call-done, bf16[2048,1024]{1,0:T(8,128)(2,1)} %param.30), kind=kOutput, calls=%fused_computation.200 | convolution fusion | flops 4294967296 | bytes 12582912 | tf_op jit(solution)/shard_map/dot_general | solution.py:86
  208.0 92.1 %all-reduce.3.cloned.1.call-done = f32[8,4,32,1024]{3,2,1,0:T(8,128)} async-done(((f32[8,4,32,1024]{3,2,1,0:T(8,128)}), f32[8,4,32,1024]{3,2,1,0:T(8,128)}) %all-reduce.3.cloned.1.call-update) | async-done | bytes 4194320
  300.2 3.0 dynamic-slice_bitcast_fusion
  303.1 4.4 all-to-all-start
  307.9 15.6 %all-to-all-done = f32[32,8,1024]{2,0,1:T(8,128)S(1)} async-done(((f32[32,8,1024]{2,0,1:T(8,128)}), f32[32,8,1024]{2,0,1:T(8,128)S(1)}, u32[]{:S(2)}, u32[]{:S(2)}) %all-to-all-start) | async-done | bytes 1048608 | tf_op jit(solution)/shard_map/all_to_all | solution.py:97
  326.7 38.1 %all_gather.27 = bf16[512,64]{1,0:T(8,128)(2,1)S(1)} all-gather(bf16[16,64]{1,0:T(8,128)(2,1)S(1)} %convolution_convert_fusion.2), channel_id=1, replica_groups=mesh['dp'=4,'seq'=8,'expert'=4] {'seq','expert'}, dimensions={0}, use_global_device_ids=true | all-gather | bytes 67584 | tf_op jit(solution)/shard_map/all_gather | solution.py:135
  364.9 12.8 %all-gather.9.cloned.1.call-done = bf16[512,8192]{1,0:T(8,128)(2,1)} async-done(((bf16[16,8192]{1,0:T(8,128)(2,1)}), bf16[512,8192]{1,0:T(8,128)(2,1)}) %all-gather.9.cloned.1.call-update) | async-done | bytes 8388624 | tf_op jit(solution)/shard_map/all_gather | solution.py:134
  377.7 8.0 %mul.821 = f32[512,64,128]{2,1,0:T(8,128)} broadcast(bf16[512,64]{1,0:T(8,128)(2,1)S(1)} %all_gather.27), dimensions={0,1} | broadcast | bytes 16842752 | tf_op jit(solution)/shard_map/mul | solution.py:140
  385.6 18.4 %fusion.89 = f32[512,384]{1,0:T(8,128)S(1)} fusion(bf16[8192,384]{1,0:T(8,128)(2,1)} %param.35, f32[64,8,64,128]{3,2,1,0:T(8,128)} %bitcast.286, bf16[512,8192]{1,0:T(8,128)(2,1)S(1)} %copy-done.1), kind=kOutput, calls=%fused_computation.199 | convolution fusion | flops 3233808384 | bytes 32243712 | tf_op jit(solution)/shard_map/dot_general | solution.py:146
  404.0 28.3 %convolution_convert_fusion = bf16[512,8192]{1,0:T(8,128)(2,1)} fusion(bf16[384,8192]{1,0:T(8,128)(2,1)} %param.37, bf16[8192,384]{1,0:T(8,128)(2,1)} %param.36, f32[512,384]{1,0:T(8,128)S(1)} %fusion.89, f32[64,8,64,128]{3,2,1,0:T(8,128)} %bitcast.287, bf16[512,8192]{1,0:T(8,128)(2,1)} %all-gather.9.cloned.1.call-done), kind=kOutput, calls=%fused_computation.137 | convolution fusion | flops 6460407808 | bytes 46923776 | tf_op jit(solution)/shard_map/dot_general | solution.py:150
  433.2 91.7 %reduce-scatter.5.cloned.1.call-done = bf16[16,8192]{1,0:T(8,128)(2,1)} async-done(((bf16[512,8192]{1,0:T(8,128)(2,1)}), bf16[16,8192]{1,0:T(8,128)(2,1)}) %reduce-scatter.5.cloned.1.call-update) | async-done | bytes 262160 | tf_op jit(solution)/shard_map/reduce_scatter | solution.py:149
  524.9 2.1 fusion.50
  (281 shorter events, 93.8 us)
Async XLA Ops:
  6.5 425.8 %copy-start = (bf16[8192,16]{0,1:T(8,128)(2,1)S(1)}, bf16[8192,16]{0,1:T(8,128)(2,1)}, u32[]{:S(2)}) copy-start(bf16[8192,16]{0,1:T(8,128)(2,1)} %param.33) | copy-start | bytes 786436
  6.5 27.9 %copy-start.7 = (bf16[16,128]{1,0:T(8,128)(2,1)S(1)}, bf16[16,128]{1,0:T(8,128)(2,1)}, u32[]{:S(2)}) copy-start(bf16[16,128]{1,0:T(8,128)(2,1)} %param.28) | copy-start | bytes 12292
  6.5 85.0 %copy-start.5 = (f32[2048]{0:T(1024)S(1)}, f32[2048]{0:T(1024)}, u32[]{:S(2)}) copy-start(f32[2048]{0:T(1024)} %param.29) | copy-start | bytes 24580
  6.5 52.3 %all-gather.13.cloned.1.call-start = ((), (), s32[]{:S(2)}) async-start(), calls=%async_computation.6 | async-start | bytes 1179648 | tf_op jit(solution)/shard_map/all_gather | solution.py:11
  32.1 0.6 copy-start.2
  32.1 130.7 %copy-start.4 = (bf16[128,2048]{1,0:T(8,128)(2,1)S(1)}, bf16[128,2048]{1,0:T(8,128)(2,1)}, u32[]{:S(2)}) copy-start(bf16[128,2048]{1,0:T(8,128)(2,1)} %param.23) | copy-start | bytes 1572868
  32.7 51.2 %all-gather.11.cloned.1.call-start = ((), (), s32[]{:S(2)}) async-start(), calls=%async_computation.5 | async-start | bytes 1179648 | tf_op jit(solution)/shard_map/all_gather | solution.py:11
  34.4 163.1 %all-gather.7.cloned.1.call-start = ((), (), s32[]{:S(2)}) async-start(), calls=%async_computation.2 | async-start | bytes 4718592 | tf_op jit(solution)/shard_map/all_gather | solution.py:87
  165.1 42.3 %copy-start.9 = (u32[128]{0:T(128)S(1)}, u32[128]{0:T(128)}, u32[]{:S(2)}) copy-start(u32[128]{0:T(128)} %constant.87) | copy-start | bytes 1540
  165.2 135.0 %all-reduce.3.cloned.1.call-start = ((), (), s32[]{:S(2)}) async-start(), calls=%async_computation.7 | async-start | bytes 8388608
  207.4 100.2 %copy-start.8 = (s32[32,2]{0,1:T(2,128)S(1)}, s32[32,2]{0,1:T(2,128)}, u32[]{:S(2)}) copy-start(s32[32,2]{0,1:T(2,128)} %param.34) | copy-start | bytes 772
  207.4 116.2 %copy-start.3 = (bf16[32,8192]{1,0:T(8,128)(2,1)S(1)}, bf16[32,8192]{1,0:T(8,128)(2,1)}, u32[]{:S(2)}) copy-start(bf16[32,8192]{1,0:T(8,128)(2,1)} %param.31) | copy-start | bytes 1572868
  207.4 116.5 %copy-start.6 = (f32[8192]{0:T(1024)S(1)}, f32[8192]{0:T(1024)}, u32[]{:S(2)}) copy-start(f32[8192]{0:T(1024)} %param.32) | copy-start | bytes 98308
  303.1 20.4 %all-to-all-start = ((f32[32,8,1024]{2,0,1:T(8,128)}), f32[32,8,1024]{2,0,1:T(8,128)S(1)}, u32[]{:S(2)}, u32[]{:S(2)}) async-start(f32[32,8,1024]{2,0,1:T(8,128)} %dynamic-slice_bitcast_fusion), calls=%async_computation | async-start | bytes 2097152 | tf_op jit(solution)/shard_map/all_to_all | solution.py:97
  307.5 70.1 %all-gather.9.cloned.1.call-start = ((), (), s32[]{:S(2)}) async-start(), calls=%async_computation.3 | async-start | bytes 8650752 | tf_op jit(solution)/shard_map/all_gather | solution.py:134
  326.6 198.3 %reduce-scatter.5.cloned.1.call-start = ((), (), s32[]{:S(2)}) async-start(), calls=%async_computation.4 | async-start | bytes 8650752 | tf_op jit(solution)/shard_map/reduce_scatter | solution.py:149
  377.7 8.0 %copy-start.1 = (bf16[512,8192]{1,0:T(8,128)(2,1)S(1)}, bf16[512,8192]{1,0:T(8,128)(2,1)}, u32[]{:S(2)}) copy-start(bf16[512,8192]{1,0:T(8,128)(2,1)} %all-gather.9.cloned.1.call-done) | copy-start | bytes 25165828
Sparse Core Ops, SparseCore 0:
  32.9 25.9 all-gather.12
  60.5 23.3 all-gather.10
  165.3 32.1 all-gather.6
  207.6 92.5 all-reduce.2
  326.7 50.9 all-gather.8
  432.5 92.3 reduce-scatter.4
where the time goes:
time: 535 us; the launch traced here: 534 us
  waiting for transfers between devices  294 us (55%)
  other arithmetic  96.1 us (18%)
  matrix products  60.5 us (11%)
  blocking collectives  38.1 us (7%)
  local copies, waits for them, and re-layouts  25.5 us (5%)
  between operations  13.7 us (3%)
    unnamed x7, waiting for transfers between devices  92.2 us
    reduce_scatter x1, waiting for transfers between devices, on_device(): lax.psum_scatter(jnp.dot(active, down_weight, preferred_element_type=jnp....  91.7 us
    reduce_sum x48, other arithmetic, scan_advance(): y_now = jnp.sum(c_now[:, None] * state, axis=0) + skip_gain * x_now  54.8 us
    all_gather x2, waiting for transfers between devices, entering(): pieces = jax.tree.map(lambda part: lax.all_gather(part, axis), value)  49.4 us
    all_gather x1, blocking collectives, on_device(): lax.all_gather(send_scale, ('seq', 'expert'), axis=0, tiled=True)  38.1 us
    all_gather x1, waiting for transfers between devices, on_device(): lax.all_gather(gated, 'seq', axis=0, tiled=True)  32.3 us
    dot_general x1, matrix products, on_device(): jnp.dot(active, down_weight, preferred_element_type=jnp.float32)  28.3 us
    add x16, other arithmetic, end_advance(): jnp.exp(-step_now[None, :] * decay_rate) * state  18.7 us
  transfers between devices with their start and end apart: 7, of which 7 were waited for; matrix products, arithmetic and copies ran while one was open for 1% of the time, Pallas kernels for 0%

commit v1 on v0

--- a/solution.py
+++ b/solution.py
@@ -4,6 +4,12 @@
 from jax.sharding import PartitionSpec as P
 
 BLOCK = 128
+
+
+def trade_parts(x, mesh_axis, split, join):
+    cells = jnp.split(x, lax.axis_size(mesh_axis), axis=split)
+    incoming = lax.all_to_all(jnp.stack(cells), mesh_axis, 0, 0)
+    return jnp.concatenate(incoming, axis=join)
 
 
 def entering(value, axis, join, neutral):
@@ -94,7 +100,7 @@
     grouped = column_part.reshape(seq_count, expert_count, rows, column_part.shape[1])
     summed = lax.psum_scatter(grouped, "expert", scatter_dimension=1, tiled=True)
     arranged = jnp.transpose(summed[:, 0], (1, 0, 2))
-    swapped = lax.all_to_all(arranged, "seq", split_axis=1, concat_axis=1, tiled=True)
+    swapped = trade_parts(arranged, "seq", 1, 1)
     mamba_out = swapped.reshape(rows, -1)
     hidden = (residual.astype(jnp.float32) + mamba_out).astype(jnp.bfloat16)
     hidden_f = hidden.astype(jnp.float32)

time: 535 us -> 540 us (level)
  no operation moved by 1% of the time
where the time goes in v1:
time: 540 us; the launch traced here: 538 us
  waiting for transfers between devices  294 us (54%)
  other arithmetic  96.2 us (18%)
  matrix products  60.4 us (11%)
  blocking collectives  38.1 us (7%)
  local copies, waits for them, and re-layouts  29.8 us (6%)
  between operations  13.7 us (3%)
    unnamed x7, waiting for transfers between devices  92.2 us
    reduce_scatter x1, waiting for transfers between devices, on_device(): lax.psum_scatter(jnp.dot(active, down_weight, preferred_element_type=jnp....  91.7 us
    reduce_sum x48, other arithmetic, scan_advance(): y_now = jnp.sum(c_now[:, None] * state, axis=0) + skip_gain * x_now  54.9 us
    all_gather x2, waiting for transfers between devices, entering(): pieces = jax.tree.map(lambda part: lax.all_gather(part, axis), value)  49.4 us
    all_gather x1, blocking collectives, on_device(): lax.all_gather(send_scale, ('seq', 'expert'), axis=0, tiled=True)  38.1 us
    all_gather x1, waiting for transfers between devices, on_device(): lax.all_gather(gated, 'seq', axis=0, tiled=True)  32.3 us
    dot_general x1, matrix products, on_device(): jnp.dot(active, down_weight, preferred_element_type=jnp.float32)  28.3 us
    add x16, other arithmetic, end_advance(): jnp.exp(-step_now[None, :] * decay_rate) * state  18.5 us
  transfers between devices with their start and end apart: 7, of which 7 were waited for; matrix products, arithmetic and copies ran while one was open for 1% of the time, Pallas kernels for 0%

profile of v1, /device:TPU:0, one launch (start us, length us, event | category | flops | bytes accessed | tf_op | source)
XLA Modules:
  0.0 538.1 jit_solution(14334320308884802448)
XLA Ops:
  8.5 1.7 fusion.67
  10.2 21.7 %while.38 = (s32[]{:T(128)}, f32[16,2048]{1,0:T(8,128)S(1)}, f32[16,8,2048]{2,1,0:T(8,128)S(1)}, f32[16,2048]{1,0:T(8,128)}, f32[16,8,2048]{2,1,0:T(8,128)S(1)},...) while((s32[]{:T(128)}, f32[16,2048]{1,0:T(8,128)S(1)}, ...), condition=%wide.region_2.3_spmd.clone, body=%wide.region_1.2_spmd.clone.sunk | while | flops 1114122 | bytes 789271 | solution.py:44
  32.6 1.6 multiply_exponential_fusion
  34.5 24.2 %all-gather.13.cloned.1.call-done = f32[128,2048]{1,0:T(8,128)} async-done(((f32[16,2048]{1,0:T(8,128)}), f32[128,2048]{1,0:T(8,128)}) %all-gather.13.cloned.1.call-update) | async-done | bytes 1048592 | tf_op jit(solution)/shard_map/all_gather | solution.py:17
  58.7 25.1 %all-gather.11.cloned.1.call-done = f32[128,2048]{1,0:T(8,128)} async-done(((f32[16,2048]{1,0:T(8,128)}), f32[128,2048]{1,0:T(8,128)}) %all-gather.11.cloned.1.call-update) | async-done | bytes 1048592 | tf_op jit(solution)/shard_map/all_gather | solution.py:17
  83.8 7.6 %while.39 = (s32[]{:T(128)}, f32[16,2048]{1,0:T(8,128)S(1)}, s32[]{:T(128)}, f32[8,16,2048]{2,1,0:T(8,128)}, f32[8,16,2048]{2,1,0:T(8,128)}, /*index=5*/s32[]{:T(128)}, s32[]{:T(128)}) while((s32[]{:T(128)}, f32[16,2048]{1,0:T(8,128)S(1)}, s32[]{:T(128)}, f32[8,16,2048]{2,1,0:T(8,128)}, f32[8,16,2048]{2,1,0:T(8,128)}, ...), condition=%wide.region_4.5_spmd.clone, body=%wide.region_3.4_spmd.clone.sunk | while | flops 131076 | bytes 524397 | solution.py:26
  91.5 71.4 %while.37 = (s32[]{:T(128)}, f32[16,2048]{1,0:T(8,128)S(1)}, f32[16,8,2048]{2,1,0:T(8,128)}, f32[16,8,2048]{2,1,0:T(8,128)S(1)}, f32[16,2048]{1,0:T(8,128)}, /*i...) while((s32[]{:T(128)}, f32[16,2048]{1,0:T(8,128)S(1)}, ...), condition=%wide.region_14.15_spmd, body=%wide.region_5.14_spmd.sunk | while | flops 2408457 | bytes 2078409 | solution.py:59
  92.7 1.2 multiply_reduce_fusion.11
  97.2 1.2 multiply_reduce_fusion.11
  101.7 1.2 multiply_reduce_fusion.11
  106.1 1.2 multiply_reduce_fusion.11
  110.6 1.2 multiply_reduce_fusion.11
  115.0 1.2 multiply_reduce_fusion.11
  124.0 1.2 multiply_reduce_fusion.11
  128.4 1.2 multiply_reduce_fusion.11
  132.9 1.2 multiply_reduce_fusion.11
  137.3 1.2 multiply_reduce_fusion.11
  141.8 1.2 multiply_reduce_fusion.11
  162.9 2.3 fusion.66
  165.3 32.3 %all-gather.7.cloned.1.call-done = bf16[1024,2048]{1,0:T(8,128)(2,1)} async-done(((bf16[128,2048]{1,0:T(8,128)(2,1)}), bf16[1024,2048]{1,0:T(8,128)(2,1)}) %all-gather.7.cloned.1.call-update) | async-done | bytes 4194320 | tf_op jit(solution)/shard_map/all_gather | solution.py:93
  197.5 9.9 %fusion.99 = f32[1024,1024]{1,0:T(8,128)} fusion(bf16[1024,2048]{1,0:T(8,128)(2,1)} %all-gather.7.cloned.1.call-done, bf16[2048,1024]{1,0:T(8,128)(2,1)} %param.30), kind=kOutput, calls=%fused_computation.216 | convolution fusion | flops 4294967296 | bytes 12582912 | tf_op jit(solution)/shard_map/dot_general | solution.py:92
  208.0 92.1 %all-reduce.3.cloned.1.call-done = f32[8,4,32,1024]{3,2,1,0:T(8,128)} async-done(((f32[8,4,32,1024]{3,2,1,0:T(8,128)}), f32[8,4,32,1024]{3,2,1,0:T(8,128)}) %all-reduce.3.cloned.1.call-update) | async-done | bytes 4194320
  300.2 2.0 dynamic-slice_bitcast_fusion
  307.4 4.4 all-to-all-start
  312.2 15.6 %all-to-all-done = f32[8,32,1,1024]{3,1,2,0:T(8,128)S(1)} async-done(((f32[8,32,1,1024]{3,1,2,0:T(8,128)}), f32[8,32,1,1024]{3,1,2,0:T(8,128)S(1)}, u32[]{:S(2)}, u32[]{:S(2)}) %all-to-all-start) | async-done | bytes 1048608 | tf_op jit(solution)/shard_map/all_to_all | solution.py:11
  331.0 38.1 %all_gather.27 = bf16[512,64]{1,0:T(8,128)(2,1)S(1)} all-gather(bf16[16,64]{1,0:T(8,128)(2,1)S(1)} %convolution_convert_fusion.2), channel_id=1, replica_groups=mesh['dp'=4,'seq'=8,'expert'=4] {'seq','expert'}, dimensions={0}, use_global_device_ids=true | all-gather | bytes 67584 | tf_op jit(solution)/shard_map/all_gather | solution.py:141
  369.2 12.8 %all-gather.9.cloned.1.call-done = bf16[512,8192]{1,0:T(8,128)(2,1)} async-done(((bf16[16,8192]{1,0:T(8,128)(2,1)}), bf16[512,8192]{1,0:T(8,128)(2,1)}) %all-gather.9.cloned.1.call-update) | async-done | bytes 8388624 | tf_op jit(solution)/shard_map/all_gather | solution.py:140
  382.0 8.0 %mul.821 = f32[512,64,128]{2,1,0:T(8,128)} broadcast(bf16[512,64]{1,0:T(8,128)(2,1)S(1)} %all_gather.27), dimensions={0,1} | broadcast | bytes 16842752 | tf_op jit(solution)/shard_map/mul | solution.py:146
  389.9 18.4 %fusion.97 = f32[512,384]{1,0:T(8,128)S(1)} fusion(bf16[8192,384]{1,0:T(8,128)(2,1)} %param.35, f32[64,8,64,128]{3,2,1,0:T(8,128)} %bitcast.323, bf16[512,8192]{1,0:T(8,128)(2,1)S(1)} %copy-done.1), kind=kOutput, calls=%fused_computation.215 | convolution fusion | flops 3233808384 | bytes 32243712 | tf_op jit(solution)/shard_map/dot_general | solution.py:152
  408.3 28.3 %convolution_convert_fusion = bf16[512,8192]{1,0:T(8,128)(2,1)} fusion(bf16[384,8192]{1,0:T(8,128)(2,1)} %param.37, bf16[8192,384]{1,0:T(8,128)(2,1)} %param.36, f32[512,384]{1,0:T(8,128)S(1)} %fusion.97, f32[64,8,64,128]{3,2,1,0:T(8,128)} %bitcast.324, bf16[512,8192]{1,0:T(8,128)(2,1)} %all-gather.9.cloned.1.call-done), kind=kOutput, calls=%fused_computation.137 | convolution fusion | flops 6460407808 | bytes 46923776 | tf_op jit(solution)/shard_map/dot_general | solution.py:156
  437.5 91.7 %reduce-scatter.5.cloned.1.call-done = bf16[16,8192]{1,0:T(8,128)(2,1)} async-done(((bf16[512,8192]{1,0:T(8,128)(2,1)}), bf16[16,8192]{1,0:T(8,128)(2,1)}) %reduce-scatter.5.cloned.1.call-update) | async-done | bytes 262160 | tf_op jit(solution)/shard_map/reduce_scatter | solution.py:155
  529.2 2.1 fusion.50
  (289 shorter events, 99.0 us)
Async XLA Ops:
  6.5 430.1 %copy-start = (bf16[8192,16]{0,1:T(8,128)(2,1)S(1)}, bf16[8192,16]{0,1:T(8,128)(2,1)}, u32[]{:S(2)}) copy-start(bf16[8192,16]{0,1:T(8,128)(2,1)} %param.33) | copy-start | bytes 786436
  6.5 27.8 %copy-start.7 = (bf16[16,128]{1,0:T(8,128)(2,1)S(1)}, bf16[16,128]{1,0:T(8,128)(2,1)}, u32[]{:S(2)}) copy-start(bf16[16,128]{1,0:T(8,128)(2,1)} %param.28) | copy-start | bytes 12292
  6.5 84.9 %copy-start.5 = (f32[2048]{0:T(1024)S(1)}, f32[2048]{0:T(1024)}, u32[]{:S(2)}) copy-start(f32[2048]{0:T(1024)} %param.29) | copy-start | bytes 24580
  6.5 52.2 %all-gather.13.cloned.1.call-start = ((), (), s32[]{:S(2)}) async-start(), calls=%async_computation.6 | async-start | bytes 1179648 | tf_op jit(solution)/shard_map/all_gather | solution.py:17
  31.9 0.6 copy-start.2
  31.9 130.9 %copy-start.4 = (bf16[128,2048]{1,0:T(8,128)(2,1)S(1)}, bf16[128,2048]{1,0:T(8,128)(2,1)}, u32[]{:S(2)}) copy-start(bf16[128,2048]{1,0:T(8,128)(2,1)} %param.23) | copy-start | bytes 1572868
  32.6 51.2 %all-gather.11.cloned.1.call-start = ((), (), s32[]{:S(2)}) async-start(), calls=%async_computation.5 | async-start | bytes 1179648 | tf_op jit(solution)/shard_map/all_gather | solution.py:17
  34.3 163.3 %all-gather.7.cloned.1.call-start = ((), (), s32[]{:S(2)}) async-start(), calls=%async_computation.2 | async-start | bytes 4718592 | tf_op jit(solution)/shard_map/all_gather | solution.py:93
  165.2 42.3 %copy-start.9 = (u32[128]{0:T(128)S(1)}, u32[128]{0:T(128)}, u32[]{:S(2)}) copy-start(u32[128]{0:T(128)} %constant.87) | copy-start | bytes 1540
  165.2 134.9 %all-reduce.3.cloned.1.call-start = ((), (), s32[]{:S(2)}) async-start(), calls=%async_computation.7 | async-start | bytes 8388608
  207.4 104.5 %copy-start.8 = (s32[32,2]{0,1:T(2,128)S(1)}, s32[32,2]{0,1:T(2,128)}, u32[]{:S(2)}) copy-start(s32[32,2]{0,1:T(2,128)} %param.34) | copy-start | bytes 772
  207.4 120.5 %copy-start.3 = (bf16[32,8192]{1,0:T(8,128)(2,1)S(1)}, bf16[32,8192]{1,0:T(8,128)(2,1)}, u32[]{:S(2)}) copy-start(bf16[32,8192]{1,0:T(8,128)(2,1)} %param.31) | copy-start | bytes 1572868
  207.4 120.8 %copy-start.6 = (f32[8192]{0:T(1024)S(1)}, f32[8192]{0:T(1024)}, u32[]{:S(2)}) copy-start(f32[8192]{0:T(1024)} %param.32) | copy-start | bytes 98308
  307.4 20.4 %all-to-all-start = ((f32[8,32,1,1024]{3,1,2,0:T(8,128)}), f32[8,32,1,1024]{3,1,2,0:T(8,128)S(1)}, u32[]{:S(2)}, u32[]{:S(2)}) async-start(f32[8,32,1,1024]{3,1,2,0:T(8,128)} %fusion.71), calls=%async_computation | async-start | bytes 2097152 | tf_op jit(solution)/shard_map/all_to_all | solution.py:11
  311.8 70.1 %all-gather.9.cloned.1.call-start = ((), (), s32[]{:S(2)}) async-start(), calls=%async_computation.3 | async-start | bytes 8650752 | tf_op jit(solution)/shard_map/all_gather | solution.py:140
  330.9 198.3 %reduce-scatter.5.cloned.1.call-start = ((), (), s32[]{:S(2)}) async-start(), calls=%async_computation.4 | async-start | bytes 8650752 | tf_op jit(solution)/shard_map/reduce_scatter | solution.py:155
  382.0 8.0 %copy-start.1 = (bf16[512,8192]{1,0:T(8,128)(2,1)S(1)}, bf16[512,8192]{1,0:T(8,128)(2,1)}, u32[]{:S(2)}) copy-start(bf16[512,8192]{1,0:T(8,128)(2,1)} %all-gather.9.cloned.1.call-done) | copy-start | bytes 25165828
Sparse Core Ops, SparseCore 0:
  32.7 25.9 all-gather.12
  60.4 23.3 all-gather.10
  165.3 32.1 all-gather.6
  207.6 92.5 all-reduce.2
  331.0 50.9 all-gather.8
  436.8 92.3 reduce-scatter.4
